TPU v7x, 256 devices: a whole 4x4x8 slice. The times are simulated.
256 devices in a mesh: rows: 32 (over y, x, core), cols: 8 (over z).
Axes of the slice: x: 4, y: 4, z: 8, core: 2. Of those that a mesh axis runs over, the one named last changes fastest.
Arguments:
- sheet: bfloat16 [16, 4096, 1024], P('cols', 'rows'), may hold values from -600 to 600
- w_in: bfloat16 [1024, 16, 384], P(None, 'cols'), may hold values from -0.1875 to 0.1875
- w_out: bfloat16 [16, 128, 1024], P('cols'), may hold values from -0.125 to 0.125
Outputs:
- mixed: bfloat16 [16, 4096, 1024], P('cols', 'rows')
All inputs are finite; a program needn't handle non-finite values.
Results may differ from a plain program's by a relative error of at most 0.0067.
Values may be sent and summed in bfloat16 or wider, within the bound.
No kernel may reach another device: no remote copies, remote signals or barrier semaphores. Data moves between devices by JAX's collectives and lax.ppermute only.
A program may use at most 128 MiB of HBM per device.

v0:
```python
import jax
import jax.numpy as jnp
import numpy as np
from jax import lax
from jax.sharding import Mesh, PartitionSpec as P

ROWS_AXES = ("y", "x", "core")


def head_norm(values):
    return values * lax.rsqrt(jnp.mean(values * values, axis=-1, keepdims=True) + 1e-06)


def feature_map(values):
    return jax.nn.elu(values) + 1.0


def finish_proj(proj):
    parts = [
        head_norm(proj[..., 0, :]),
        head_norm(proj[..., 1, :]),
        proj[..., 2, :],
        feature_map(proj[..., 3, :]),
        feature_map(proj[..., 4, :]),
        proj[..., 5, :],
    ]
    return jnp.stack(parts, axis=-2).astype(jnp.bfloat16)


def masked_prefix(gathered, mine):
    idx = lax.broadcasted_iota(jnp.int32, gathered.shape, 0)
    before = jnp.sum(jnp.where(idx < mine, gathered, 0.0), axis=0)
    return (before, jnp.sum(gathered, axis=0))


def exclusive_rows_scan(states):
    core = lax.axis_index("core")
    pair = lax.all_gather(states, "core")
    total = pair[0] + pair[1]
    own = jnp.where(core == 1, pair[0], jnp.zeros_like(pair[0]))
    half = total.shape[0] // 2
    mine = lax.dynamic_slice_in_dim(total, core * half, half, axis=0)
    gx = lax.all_gather(mine, "x")
    xpre, xsum = masked_prefix(gx, lax.axis_index("x"))
    gy = lax.all_gather(xsum, "y")
    ypre, _ = masked_prefix(gy, lax.axis_index("y"))
    chip_prefix = lax.all_gather(ypre + xpre, "core", axis=0, tiled=True)
    return chip_prefix + own


def body(sheet, w_in, w_out):
    high = lax.Precision.HIGHEST
    width = sheet.shape[2]
    heads_here = w_in.shape[1]
    hdim = w_out.shape[1] // 2
    ncols = lax.axis_size("cols")
    core = lax.axis_index("core")
    wh = width // 2
    w_part = lax.dynamic_slice_in_dim(w_out, core * wh, wh, axis=2)
    w_part = lax.all_gather(w_part, "cols", axis=0, tiled=True)
    w_full = lax.all_gather(w_part, "core", axis=2, tiled=True)
    xloc = sheet.astype(jnp.float32)
    normed = (xloc * lax.rsqrt(jnp.mean(xloc * xloc, axis=-1, keepdims=True) + 1e-06)).astype(
        jnp.bfloat16
    )
    piece = lax.all_gather(normed, "cols", axis=0, tiled=True)
    w_flat = w_in.reshape(width, heads_here * 6 * hdim)
    proj = jnp.dot(piece.reshape(-1, width), w_flat, preferred_element_type=jnp.float32)
    all_cols, row_count = (piece.shape[0], piece.shape[1])
    parts = finish_proj(proj.reshape(all_cols, row_count, heads_here, 6, hdim))
    qrow, krow, vrow = (parts[:, :, :, 0], parts[:, :, :, 1], parts[:, :, :, 2])
    fq, fk, vcol = (parts[:, :, :, 3], parts[:, :, :, 4], parts[:, :, :, 5])
    states = jnp.einsum("crhk,crhv->chkv", fk, vcol, preferred_element_type=jnp.float32)
    prior = exclusive_rows_scan(states)
    scale = hdim ** (-0.5)
    score = jnp.einsum("crhd,erhd->rhce", qrow, krow, preferred_element_type=jnp.float32) * scale
    expo = jnp.exp(score)
    weights = (expo / jnp.sum(expo, axis=-1, keepdims=True)).astype(jnp.bfloat16)
    orow = jnp.einsum("rhce,erhd->crhd", weights, vrow, preferred_element_type=jnp.float32).astype(
        jnp.bfloat16
    )
    causal = (jnp.arange(row_count)[:, None] >= jnp.arange(row_count)[None, :]).astype(jnp.float32)
    inner = jnp.einsum("cthd,cshd->chts", fq, fk, preferred_element_type=jnp.float32) * causal
    local = jnp.einsum("chts,cshv->cthv", inner, vcol.astype(jnp.float32), precision=high)
    carried = jnp.einsum("cthk,chkv->cthv", fq.astype(jnp.float32), prior, precision=high)
    ocol = head_norm(carried + local).astype(jnp.bfloat16)
    results = jnp.concatenate([orow, ocol], axis=3)
    mine = lax.all_to_all(results, "cols", 0, 2, tiled=True)
    own_cols = mine.shape[0]
    mixed = jnp.dot(
        mine.reshape(own_cols * row_count, -1),
        w_full.reshape(-1, width),
        preferred_element_type=jnp.float32,
    )
    return mixed.reshape(own_cols, row_count, width).astype(jnp.bfloat16)


def split_mesh(mesh):
    devs = mesh.devices
    n_rows, n_cols = devs.shape
    try:
        nx = len({d.coords[0] for d in devs.flat})
    except Exception:
        nx = 4
    ny = n_rows // (nx * 2)
    return Mesh(devs.reshape(ny, nx, 2, n_cols), ROWS_AXES + ("cols",))


def solution(mesh):
    m4 = split_mesh(mesh)
    spec = P("cols", ROWS_AXES, None)
    return jax.shard_map(
        body,
        mesh=m4,
        in_specs=(spec, P(None, "cols", None), P("cols", None, None)),
        out_specs=spec,
        check_vma=False,
    )
```

profile of v0, /device:TPU:2, one launch (start us, length us, event | category | flops | bytes accessed | tf_op | source)
XLA Modules:
  0.0 267.3 jit_solution(8593396329968372122)
XLA Ops:
  6.5 0.0 copy-start
  6.5 0.0 all-gather.10.cloned.1.call-start
  6.5 1.3 fusion.10
  7.8 2.0 fusion.11
  9.8 0.0 all-gather.10.cloned.1.call-update
  9.8 0.0 all-gather.16.cloned.1.call-start
  9.9 1.7 copy.59
  11.6 1.6 copy.38
  13.3 54.4 %all-gather.10.cloned.1.call-done = bf16[16,128,1024]{2,1,0:T(8,128)(2,1)} async-done(((bf16[2,128,1024]{2,1,0:T(8,128)(2,1)}), bf16[16,128,1024]{2,1,0:T(8,128)(2,1)}) %all-gather.10.cloned.1.call-update) | async-done | bytes 4194320 | tf_op jit(solution)/shard_map/all_gather | solution.py:66
  67.7 5.8 %fusion.43 = (bf16[16,128,2,6,64]{1,4,3,2,0:T(8,128)(2,1)S(1)}, f32[16,128,2,6,64]{1,4,3,2,0:T(8,128)S(1)}) fusion(bf16[2,6,64,1024,1]{3,2,1,0,4:T(8,128)(2,1)} %bitcast.62, bf16[16,128,1024]{2,1,0:T(8,128)(2,1)} %all-gather.10.cloned.1.call-done), kind=kOutput, calls=%fused_computation.67 | convolution fusion | flops 3222798336 | bytes 15204352 | tf_op jit(solution)/shard_map/dot_general | solution.py:68
  73.5 0.0 copy-start.2
  73.5 0.0 copy-start.5
  73.5 2.6 copy-done.2
  76.2 1.0 copy-done.5
  77.1 1.5 fusion.26
  78.7 0.0 all-gather.16.cloned.1.call-update
  78.7 0.0 all-gather.20.cloned.1.call-start
  78.7 14.6 %all-gather.16.cloned.1.call-done = f32[32,2,64,64]{3,2,1,0:T(8,128)} async-done(((f32[16,2,64,64]{3,2,1,0:T(8,128)}), f32[32,2,64,64]{3,2,1,0:T(8,128)}) %all-gather.16.cloned.1.call-update) | async-done | bytes 1048592 | tf_op jit(solution)/shard_map/all_gather | solution.py:38
  93.4 1.7 fusion.42
  95.0 0.9 dynamic-slice_add_fusion
  95.9 0.0 all-gather.20.cloned.1.call-update
  95.9 0.0 all-gather.12.cloned.1.call-start
  96.0 0.0 copy-done
  96.0 0.8 constant_dynamic-slice_fusion
  96.7 0.0 all-gather.12.cloned.1.call-update
  96.8 0.0 all-gather.18.cloned.1.call-start
  96.8 32.9 %all-gather.20.cloned.1.call-done = f32[32,2,64,64]{3,2,1,0:T(8,128)} async-done(((f32[8,2,64,64]{3,2,1,0:T(8,128)}), f32[32,2,64,64]{3,2,1,0:T(8,128)}) %all-gather.20.cloned.1.call-update) | async-done | bytes 1048592 | tf_op jit(solution)/shard_map/all_gather | solution.py:43
  129.7 3.1 %select_reduce_fusion = (f32[8,2,64,64]{3,2,1,0:T(8,128)}, f32[8,2,64,64]{3,2,1,0:T(8,128)}) fusion(f32[4,8,2,64,64]{4,3,2,1,0:T(8,128)} %bitcast.59, pred[4]{0:T(512)(128)(4,1)S(1)} %iota_compare_fusion.1), kind=kLoop, calls=%fused_computation.8 | loop fusion | flops 655360 | bytes 1572868 | tf_op jit(solution)/shard_map/reduce_sum | solution.py:32
  132.8 0.0 all-gather.18.cloned.1.call-update
  132.8 0.2 all-gather.14.cloned.1.call-start
  133.1 40.2 %all-gather.12.cloned.1.call-done = bf16[16,128,512]{2,1,0:T(8,128)(2,1)} async-done(((bf16[2,128,512]{2,1,0:T(8,128)(2,1)}), bf16[16,128,512]{2,1,0:T(8,128)(2,1)}) %all-gather.12.cloned.1.call-update) | async-done | bytes 2097168 | tf_op jit(solution)/shard_map/all_gather | solution.py:60
  173.3 0.0 all-gather.14.cloned.1.call-update
  173.3 1.9 multiply_reduce_fusion.1
  175.2 1.1 slice_bitcast_fusion.1
  176.3 1.9 fusion.21
  178.2 2.5 copy.43
  180.7 2.5 copy.44
  183.2 2.2 fusion.44
  185.5 1.3 copy.45
  186.8 0.1 fusion.27
  186.9 0.1 divide_convert_fusion
  187.0 1.4 copy.47
  188.4 1.6 copy.46
  190.1 1.7 fusion.45
  191.7 3.0 %copy.48 = bf16[128,2,64,16]{0,2,1,3:T(8,128)(2,1)} copy(bf16[128,2,64,16]{2,3,1,0:T(8,128)(2,1)} %fusion.45) | data formatting | bytes 1048576 | tf_op jit(solution)/shard_map/rhce,erhd->crhd/dot_general | solution.py:79
  194.7 2.6 fusion.37
  197.4 0.0 copy-start.3
  197.4 9.5 %all-gather.18.cloned.1.call-done = f32[32,2,64,64]{3,2,1,0:T(8,128)} async-done(((f32[8,2,64,64]{3,2,1,0:T(8,128)}), f32[32,2,64,64]{3,2,1,0:T(8,128)}) %all-gather.18.cloned.1.call-update) | async-done | bytes 1048592 | tf_op jit(solution)/shard_map/all_gather | solution.py:45
  206.9 2.0 select_reduce_fusion.1
  208.8 0.0 copy-start.1
  208.8 0.0 copy-done.3
  208.8 0.1 add.72
  208.9 2.9 %all_gather.34 = f32[16,2,64,64]{3,2,1,0:T(8,128)S(1)} all-gather(f32[8,2,64,64]{3,2,1,0:T(8,128)S(1)} %add.72), channel_id=1, replica_groups=mesh['y'=4,'x'=4,'core'=2,'cols'=8] {'core'}, dimensions={0}, use_global_device_ids=true | all-gather | bytes 786432 | tf_op jit(solution)/shard_map/all_gather | solution.py:47
  211.8 0.0 copy-done.1
  211.8 2.6 fusion.18
  214.4 3.3 %multiply_reduce_fusion = (f32[16,128,2]{1,2,0:T(2,128)S(1)}, f32[16,128,2,64]{1,3,2,0:T(8,128)S(1)}) fusion(f32[16,2,64,128]{3,2,1,0:T(8,128)S(1)} %fusion.18, f32[16,2,128,128]{3,2,1,0:T(8,128)S(1)} %fusion.37, f32[128,128]{1,0:T(8,128)S(1)} %fusion.28, bf16[16,128,2,6,64]{1,4,3,2,0:T(8,128)(2,1)} %copy-done.5), kind=kOutput, calls=%fused_computation.28 | convolution fusion | flops 403959808 | bytes 4800512 | tf_op jit(solution)/shard_map/chts,cshv->cthv/dot_general | solution.py:84
  217.8 0.1 multiply_convert_fusion
  217.9 0.1 pad_maximum_fusion
  218.0 0.8 copy.53
  218.8 35.8 %all_to_all.15 = bf16[16,128,2,128]{3,2,1,0:T(2,128)(2,1)S(1)} all-to-all(bf16[16,128,2,128]{3,2,1,0:T(2,128)(2,1)S(1)} %copy.53), channel_id=1, replica_groups=mesh['y'=4,'x'=4,'core'=2,'cols'=8] {'cols'}, dimensions={0} | all-to-all | bytes 2097152 | tf_op jit(solution)/shard_map/all_to_all | solution.py:88
  254.7 0.7 copy.76
  255.4 0.8 dot_general.39
  256.2 0.0 all-gather.14.cloned.1.call-done
  256.3 4.2 %convolution_convert_fusion = bf16[2,128,1024]{2,1,0:T(8,128)(2,1)} fusion(bf16[2,128,2048]{2,1,0:T(8,128)(2,1)S(1)} %dot_general.39, bf16[2048,1024,1]{1,0,2:T(8,128)(2,1)} %bitcast.63), kind=kOutput, calls=%fused_computation.14 | convolution fusion | flops 1074003968 | bytes 5767168 | tf_op jit(solution)/shard_map/dot_general | solution.py:90
  (11 shorter events, 0.1 us)
Async XLA Ops:
  6.5 89.4 %copy-start = (bf16[2,128,1024]{2,1,0:T(8,128)(2,1)S(1)}, bf16[2,128,1024]{2,1,0:T(8,128)(2,1)}, u32[]{:S(2)}) copy-start(bf16[2,128,1024]{2,1,0:T(8,128)(2,1)} %param.5) | copy-start | bytes 1572868
  6.5 61.2 %all-gather.10.cloned.1.call-start = ((), (), s32[]{:S(2)}) async-start(), calls=%async_computation.1 | async-start | bytes 4718592 | tf_op jit(solution)/shard_map/all_gather | solution.py:66
  9.8 83.5 %all-gather.16.cloned.1.call-start = ((), (), s32[]{:S(2)}) async-start(), calls=%async_computation.4 | async-start | bytes 3145728 | tf_op jit(solution)/shard_map/all_gather | solution.py:38
  73.5 2.7 copy-start.2
  73.5 3.6 %copy-start.5 = (bf16[16,128,2,6,64]{1,4,3,2,0:T(8,128)(2,1)}, bf16[16,128,2,6,64]{1,4,3,2,0:T(8,128)(2,1)S(1)}, u32[]{:S(2)}) copy-start(bf16[16,128,2,6,64]{1,4,3,2,0:T(8,128)(2,1)S(1)} %get-tuple-element.13) | copy-start | bytes 9437188
  78.7 51.0 %all-gather.20.cloned.1.call-start = ((), (), s32[]{:S(2)}) async-start(), calls=%async_computation.6 | async-start | bytes 2621440 | tf_op jit(solution)/shard_map/all_gather | solution.py:43
  95.9 77.3 %all-gather.12.cloned.1.call-start = ((), (), s32[]{:S(2)}) async-start(), calls=%async_computation.2 | async-start | bytes 2359296 | tf_op jit(solution)/shard_map/all_gather | solution.py:60
  96.8 110.1 %all-gather.18.cloned.1.call-start = ((), (), s32[]{:S(2)}) async-start(), calls=%async_computation.5 | async-start | bytes 2621440 | tf_op jit(solution)/shard_map/all_gather | solution.py:45
  132.8 123.4 %all-gather.14.cloned.1.call-start = ((), (), s32[]{:S(2)}) async-start(), calls=%async_computation.3 | async-start | bytes 6291456 | tf_op jit(solution)/shard_map/all_gather | solution.py:61
  197.4 11.5 %copy-start.3 = (f32[8,2,64,64]{3,2,1,0:T(8,128)S(1)}, f32[8,2,64,64]{3,2,1,0:T(8,128)}, u32[]{:S(2)}) copy-start(f32[8,2,64,64]{3,2,1,0:T(8,128)} %get-tuple-element.7) | copy-start | bytes 786436
  208.8 3.0 %copy-start.1 = (f32[32,2,64,64]{3,2,1,0:T(8,128)S(1)}, f32[32,2,64,64]{3,2,1,0:T(8,128)}, u32[]{:S(2)}) copy-start(f32[32,2,64,64]{3,2,1,0:T(8,128)} %all-gather.16.cloned.1.call-done) | copy-start | bytes 3145732
  214.4 3.5 %copy-start.4 = (bf16[128,2,64,16]{0,2,1,3:T(8,128)(2,1)S(1)}, bf16[128,2,64,16]{0,2,1,3:T(8,128)(2,1)}, u32[]{:S(2)}) copy-start(bf16[128,2,64,16]{0,2,1,3:T(8,128)(2,1)} %copy.48) | copy-start | bytes 1572868
Sparse Core Ops, SparseCore 0:
  10.0 57.6 all-gather.9
  78.8 14.5 all-gather.15
  96.0 33.6 all-gather.19
  131.4 41.8 all-gather.11
  174.9 31.8 all-gather.17
  208.5 19.0 all-gather.13
where the time goes:
time: 268 us; the launch traced here: 267 us
  waiting for transfers between devices  152 us (57%)
  blocking collectives  38.7 us (14%)
  local copies, waits for them, and re-layouts  25.3 us (9%)
  matrix products  24 us (9%)
  between operations  13.8 us (5%)
  other arithmetic  13.4 us (5%)
    all_gather x1, waiting for transfers between devices, body(): piece = lax.all_gather(normed, 'cols', axis=0, tiled=True)  54.4 us
    all_gather x1, waiting for transfers between devices, body(): w_part = lax.all_gather(w_part, 'cols', axis=0, tiled=True)  40.2 us
    all_to_all x1, blocking collectives, body(): mine = lax.all_to_all(results, 'cols', 0, 2, tiled=True)  35.8 us
    all_gather x1, waiting for transfers between devices, exclusive_rows_scan(): gx = lax.all_gather(mine, 'x')  32.9 us
    all_gather x1, waiting for transfers between devices, exclusive_rows_scan(): pair = lax.all_gather(states, 'core')  14.6 us
    all_gather x1, waiting for transfers between devices, exclusive_rows_scan(): gy = lax.all_gather(xsum, 'y')  9.49 us
    squeeze x4, local copies, waits for them, and re-layouts, body(): qrow, krow, vrow = (parts[:, :, :, 0], parts[:, :, :, 1], parts[:, :, :, 2])  7.74 us
    dot_general x1, matrix products, body(): jnp.dot(piece.reshape(-1, width), w_flat, preferred_element_type=jnp.floa...  5.78 us
  transfers between devices with their start and end apart: 6, of which 5 were waited for; matrix products, arithmetic and copies ran while one was open for 16% of the time, Pallas kernels for 0%

commit v1 on v0

--- a/solution.py
+++ b/solution.py
@@ -5,6 +5,19 @@
 from jax.sharding import Mesh, PartitionSpec as P
 
 ROWS_AXES = ("y", "x", "core")
+
+
+def collect(x, axis, dim):
+    ways = lax.axis_size(axis)
+    up = [(d, (d + 1) % ways) for d in range(ways)]
+    down = [(d, (d - 1) % ways) for d in range(ways)]
+    earlier, later = ([x], [x])
+    for _ in range(ways // 2):
+        earlier.append(lax.ppermute(earlier[-1], axis, up))
+    for _ in range((ways - 1) // 2):
+        later.append(lax.ppermute(later[-1], axis, down))
+    line = jnp.concatenate([*earlier[::-1], *later[1:]], axis=dim)
+    return jnp.roll(line, (lax.axis_index(axis) - ways // 2) * x.shape[dim], axis=dim)
 
 
 def head_norm(values):
@@ -57,7 +70,7 @@
     core = lax.axis_index("core")
     wh = width // 2
     w_part = lax.dynamic_slice_in_dim(w_out, core * wh, wh, axis=2)
-    w_part = lax.all_gather(w_part, "cols", axis=0, tiled=True)
+    w_part = collect(w_part, "cols", 0)
     w_full = lax.all_gather(w_part, "core", axis=2, tiled=True)
     xloc = sheet.astype(jnp.float32)
     normed = (xloc * lax.rsqrt(jnp.mean(xloc * xloc, axis=-1, keepdims=True) + 1e-06)).astype(

time: 268 us -> 230 us (0.86)
  waiting for transfers between devices: 152 us -> 90.7 us
  local copies, waits for them, and re-layouts: 25.3 us -> 38.2 us
  starting transfers between devices: 0.39 us -> 10.4 us
    all_gather x1 -> x0, waiting for transfers between devices: 40.2 us -> none  [body(): w_part = lax.all_gather(w_part, 'cols', axis=0, tiled=True)]
    all_gather x1, waiting for transfers between devices: 32.9 us -> 3.29 us  [exclusive_rows_scan(): gx = lax.all_gather(mine, 'x')]
    ppermute x0 -> x7, waiting for transfers between devices: none -> 17.5 us  [the longest x4 17.5 us: collect(): earlier.append(lax.ppermute(earlier[-1], axis, up))]
    unnamed x13 -> x30, local copies, waits for them, and re-layouts: 5.35 us -> 16.3 us
    ppermute x0 -> x7, starting transfers between devices: none -> 10.1 us  [the longest x3 8.36 us: collect(): later.append(lax.ppermute(later[-1], axis, down))]
    all_gather x1, waiting for transfers between devices: 9.49 us -> 0.01 us  [exclusive_rows_scan(): gy = lax.all_gather(xsum, 'y')]
    dynamic_slice x0 -> x1, local copies, waits for them, and re-layouts: none -> 3.08 us  [collect(): jnp.roll(line, (lax.axis_index(axis) - ways // 2) * x.shape[dim], axis=dim)]
  transfers between devices with their start and end apart: 6 -> 12, of which waited for: 5 -> 6; matrix products, arithmetic and copies ran while one was open for 16% -> 25% of each run, Pallas kernels for 0% -> 0%
where the time goes in v1:
time: 230 us; the launch traced here: 229 us
  waiting for transfers between devices  90.7 us (39%)
  blocking collectives  38.8 us (17%)
  local copies, waits for them, and re-layouts  38.2 us (17%)
  matrix products  23.8 us (10%)
  other arithmetic  13.5 us (6%)
  between operations  13.5 us (6%)
  starting transfers between devices  10.4 us (5%)
    all_gather x1, waiting for transfers between devices, body(): piece = lax.all_gather(normed, 'cols', axis=0, tiled=True)  55.3 us
    all_to_all x1, blocking collectives, body(): mine = lax.all_to_all(results, 'cols', 0, 2, tiled=True)  35.8 us
    ppermute x4, waiting for transfers between devices, collect(): earlier.append(lax.ppermute(earlier[-1], axis, up))  17.5 us
    unnamed x30, local copies, waits for them, and re-layouts  16.3 us
    all_gather x1, waiting for transfers between devices, exclusive_rows_scan(): pair = lax.all_gather(states, 'core')  14.5 us
    squeeze x4, local copies, waits for them, and re-layouts, body(): qrow, krow, vrow = (parts[:, :, :, 0], parts[:, :, :, 1], parts[:, :, :, 2])  8.56 us
    ppermute x3, starting transfers between devices, collect(): later.append(lax.ppermute(later[-1], axis, down))  8.36 us
    dot_general x1, matrix products, body(): jnp.dot(piece.reshape(-1, width), w_flat, preferred_element_type=jnp.floa...  5.38 us
  transfers between devices with their start and end apart: 12, of which 6 were waited for; matrix products, arithmetic and copies ran while one was open for 25% of the time, Pallas kernels for 0%

profile of v1, /device:TPU:2, one launch (start us, length us, event | category | flops | bytes accessed | tf_op | source)
XLA Modules:
  0.0 228.8 jit_solution(2684376724711382173)
XLA Ops:
  6.5 1.2 fusion.10
  7.8 2.0 fusion.11
  9.8 1.7 copy.59
  11.6 0.8 copy.38
  12.3 55.3 %all-gather.9.cloned.1.call-done = bf16[16,128,1024]{2,1,0:T(8,128)(2,1)} async-done(((bf16[2,128,1024]{2,1,0:T(8,128)(2,1)}), bf16[16,128,1024]{2,1,0:T(8,128)(2,1)}) %all-gather.9.cloned.1.call-update) | async-done | bytes 4194320 | tf_op jit(solution)/shard_map/all_gather | solution.py:79
  67.6 5.4 %fusion.43 = (bf16[16,128,2,6,64]{1,4,3,2,0:T(8,128)(2,1)S(1)}, f32[16,128,2,6,64]{1,4,3,2,0:T(8,128)S(1)}) fusion(bf16[2,6,64,1024,1]{3,2,1,0,4:T(8,128)(2,1)S(1)} %bitcast.62, bf16[16,128,1024]{2,1,0:T(8,128)(2,1)} %all-gather.9.cloned.1.call-done), kind=kOutput, calls=%fused_computation.84 | convolution fusion | flops 3222798336 | bytes 15204352 | tf_op jit(solution)/shard_map/dot_general | solution.py:81
  73.1 2.6 %copy-done.1 = f32[16,128,2,6,64]{1,4,3,2,0:T(8,128)} copy-done((f32[16,128,2,6,64]{1,4,3,2,0:T(8,128)}, f32[16,128,2,6,64]{1,4,3,2,0:T(8,128)S(1)}, u32[]{:S(2)}) %copy-start.1) | copy-done | bytes 6291480
  75.7 1.0 copy-done.6
  76.7 1.5 fusion.26
  78.4 0.1 collective-permute-start
  78.5 14.5 %all-gather.13.cloned.1.call-done = f32[32,2,64,64]{3,2,1,0:T(8,128)} async-done(((f32[16,2,64,64]{3,2,1,0:T(8,128)}), f32[32,2,64,64]{3,2,1,0:T(8,128)}) %all-gather.13.cloned.1.call-update) | async-done | bytes 1048592 | tf_op jit(solution)/shard_map/all_gather | solution.py:51
  92.9 1.7 fusion.42
  94.6 0.9 dynamic-slice_add_fusion
  95.6 1.6 collective-permute-start.1
  97.2 1.8 collective-permute-start.4
  99.0 6.7 %collective-permute-done.1 = bf16[2,128,512]{2,1,0:T(8,128)(2,1)S(1)} collective-permute-done((bf16[2,128,512]{2,1,0:T(8,128)(2,1)S(1)}, bf16[2,128,512]{2,1,0:T(8,128)(2,1)S(1)}, u32[]{:S(2)}, u32[]{:S(2)}) %collective-permute-start.1) | collective-permute-done | bytes 262176 | tf_op jit(solution)/shard_map/ppermute | solution.py:16
  105.7 3.2 %collective-permute-start.5 = (bf16[2,128,512]{2,1,0:T(8,128)(2,1)S(1)}, bf16[2,128,512]{2,1,0:T(8,128)(2,1)S(1)}, u32[]{:S(2)}, u32[]{:S(2)}) collective-permute-start(bf16[2,128,512]{2,1,0:T(8,128)(2,1)S(1)} %collective-permute-done.4), channel_id=1, source_target_pairs={{0,7},{1,0},{2,1},{3,2},{4,3},{5,4},{6,5},{7,6},{8,15},{9,8},{10,9... | collective-permute-start | bytes 786440 | tf_op jit(solution)/shard_map/ppermute | solution.py:18
  108.9 5.9 %collective-permute-done.2 = bf16[2,128,512]{2,1,0:T(8,128)(2,1)S(1)} collective-permute-done((bf16[2,128,512]{2,1,0:T(8,128)(2,1)S(1)}, bf16[2,128,512]{2,1,0:T(8,128)(2,1)S(1)}, u32[]{:S(2)}, u32[]{:S(2)}) %collective-permute-start.2) | collective-permute-done | bytes 262176 | tf_op jit(solution)/shard_map/ppermute | solution.py:16
  114.9 3.3 %collective-permute-start.6 = (bf16[2,128,512]{2,1,0:T(8,128)(2,1)S(1)}, bf16[2,128,512]{2,1,0:T(8,128)(2,1)S(1)}, u32[]{:S(2)}, u32[]{:S(2)}) collective-permute-start(bf16[2,128,512]{2,1,0:T(8,128)(2,1)S(1)} %collective-permute-done.5), channel_id=1, source_target_pairs={{0,7},{1,0},{2,1},{3,2},{4,3},{5,4},{6,5},{7,6},{8,15},{9,8},{10,9... | collective-permute-start | bytes 786440 | tf_op jit(solution)/shard_map/ppermute | solution.py:18
  118.2 4.9 %collective-permute-done.3 = bf16[2,128,512]{2,1,0:T(8,128)(2,1)S(1)} collective-permute-done((bf16[2,128,512]{2,1,0:T(8,128)(2,1)S(1)}, bf16[2,128,512]{2,1,0:T(8,128)(2,1)S(1)}, u32[]{:S(2)}, u32[]{:S(2)}) %collective-permute-start.3) | collective-permute-done | bytes 262176 | tf_op jit(solution)/shard_map/ppermute | solution.py:16
  123.1 0.7 constant_dynamic-update-slice_fusion.15
  123.8 0.7 constant_dynamic-update-slice_fusion.14
  124.6 0.7 constant_dynamic-update-slice_fusion.13
  125.3 0.7 constant_dynamic-update-slice_fusion.12
  126.0 3.3 %all-gather.17.cloned.1.call-done = f32[32,2,64,64]{3,2,1,0:T(8,128)} async-done(((f32[8,2,64,64]{3,2,1,0:T(8,128)}), f32[32,2,64,64]{3,2,1,0:T(8,128)}) %all-gather.17.cloned.1.call-update) | async-done | bytes 1048592 | tf_op jit(solution)/shard_map/all_gather | solution.py:56
  129.3 3.1 %select_reduce_fusion = (f32[8,2,64,64]{3,2,1,0:T(8,128)}, f32[8,2,64,64]{3,2,1,0:T(8,128)}) fusion(f32[4,8,2,64,64]{4,3,2,1,0:T(8,128)} %bitcast.58, pred[4]{0:T(512)(128)(4,1)S(1)} %iota_compare_fusion.1), kind=kLoop, calls=%fused_computation.8 | loop fusion | flops 655360 | bytes 1572868 | tf_op jit(solution)/shard_map/reduce_sum | solution.py:45
  132.4 0.2 all-gather.11.cloned.1.call-start
  132.7 0.7 constant_dynamic-update-slice_fusion.11
  133.4 0.7 constant_dynamic-update-slice_fusion.10
  134.1 0.7 constant_dynamic-update-slice_fusion.9
  134.8 0.7 constant_dynamic-update-slice_fusion.8
  135.6 0.7 constant_dynamic-update-slice_fusion.7
  136.3 0.8 constant_dynamic-update-slice_fusion.6
  137.1 0.7 constant_dynamic-update-slice_fusion.5
  137.8 0.7 constant_dynamic-update-slice_fusion.4
  138.6 0.7 constant_dynamic-update-slice_fusion.3
  139.3 0.7 constant_dynamic-update-slice_fusion.2
  140.0 0.7 constant_dynamic-update-slice_fusion.1
  140.7 0.7 constant_dynamic-update-slice_fusion
  141.5 3.1 %constant_dynamic-slice_fusion = bf16[16,128,512]{2,1,0:T(8,128)(2,1)} fusion(bf16[32,128,512]{2,1,0:T(8,128)(2,1)} %constant_dynamic-update-slice_fusion, s32[]{:T(128)S(6)} %select_n.69), kind=kLoop, calls=%fused_computation.75 | loop fusion | bytes 4194308 | tf_op jit(solution)/shard_map/jit(_roll_dynamic)/dynamic_slice | solution.py:20
  144.6 2.0 multiply_reduce_fusion.1
  146.6 1.9 slice_bitcast_fusion.1
  148.6 1.9 fusion.21
  150.5 1.6 copy.43
  152.1 2.5 %copy.44 = bf16[16,128,2,64]{3,0,2,1:T(8,128)(2,1)} copy(bf16[16,128,2,64]{1,3,2,0:T(8,128)(2,1)S(1)} %get-tuple-element.9) | data formatting | bytes 1048576 | tf_op jit(solution)/shard_map/squeeze | solution.py:84
  154.7 1.9 fusion.44
  156.6 1.3 copy.45
  158.1 1.4 copy.47
  159.5 2.5 %copy.46 = bf16[16,128,2,64]{3,0,2,1:T(8,128)(2,1)S(1)} copy(bf16[16,128,2,64]{1,3,2,0:T(8,128)(2,1)} %slice_bitcast_fusion.1) | data formatting | bytes 1048576 | tf_op jit(solution)/shard_map/squeeze | solution.py:84
  162.0 0.7 fusion.45
  162.7 1.8 copy.48
  164.5 4.1 %fusion.37 = f32[16,2,128,128]{3,2,1,0:T(8,128)} fusion(f32[16,128,2,6,64]{1,4,3,2,0:T(8,128)} %copy-done.1), kind=kOutput, calls=%fused_computation.82 | convolution fusion | flops 69730304 | bytes 4194304 | tf_op jit(solution)/shard_map/cthd,cshd->chts/dot_general | solution.py:96
  168.6 2.0 select_reduce_fusion.1
  170.6 0.1 add.83
  170.7 2.9 %all_gather.31 = f32[16,2,64,64]{3,2,1,0:T(8,128)S(1)} all-gather(f32[8,2,64,64]{3,2,1,0:T(8,128)S(1)} %add.83), channel_id=1, replica_groups=mesh['y'=4,'x'=4,'core'=2,'cols'=8] {'core'}, dimensions={0}, use_global_device_ids=true | all-gather | bytes 786432 | tf_op jit(solution)/shard_map/all_gather | solution.py:60
  173.6 2.6 %fusion.18 = f32[16,2,64,128]{3,2,1,0:T(8,128)S(1)} fusion(f32[16,2,64,64]{3,2,1,0:T(8,128)S(1)} %all_gather.31, pred[]{:T(512)S(6)} %eq.6, f32[32,2,64,64]{3,2,1,0:T(8,128)S(1)} %copy-done, f32[16,128,2,6,64]{1,4,3,2,0:T(8,128)} %copy-done.1), kind=kOutput, calls=%fused_computation.26 | convolution fusion | flops 202899456 | bytes 4194305 | tf_op jit(solution)/shard_map/cthk,chkv->cthv/dot_general | solution.py:98
  176.2 3.3 %multiply_reduce_fusion = (f32[16,128,2]{1,2,0:T(2,128)S(1)}, f32[16,128,2,64]{1,3,2,0:T(8,128)S(1)}) fusion(f32[16,2,64,128]{3,2,1,0:T(8,128)S(1)} %fusion.18, f32[16,2,128,128]{3,2,1,0:T(8,128)S(1)} %copy-done.2, f32[128,128]{1,0:T(8,128)S(1)} %fusion.28, bf16[16,128,2,6,64]{1,4,3,2,0:T(8,128)(2,1)} %copy-done.6), kind=kOutput, calls=%fused_computation.28 | convolution fusion | flops 403959808 | bytes 4800512 | tf_op jit(solution)/shard_map/chts,cshv->cthv/dot_general | solution.py:97
  179.6 0.1 multiply_convert_fusion
  179.7 0.1 pad_maximum_fusion
  179.8 0.8 copy.53
  180.6 35.8 %all_to_all.15 = bf16[16,128,2,128]{3,2,1,0:T(2,128)(2,1)S(1)} all-to-all(bf16[16,128,2,128]{3,2,1,0:T(2,128)(2,1)S(1)} %copy.53), channel_id=1, replica_groups=mesh['y'=4,'x'=4,'core'=2,'cols'=8] {'cols'}, dimensions={0} | all-to-all | bytes 2097152 | tf_op jit(solution)/shard_map/all_to_all | solution.py:101
  216.5 0.7 copy.76
  217.2 0.8 dot_general.39
  218.1 4.2 %convolution_convert_fusion = bf16[2,128,1024]{2,1,0:T(8,128)(2,1)} fusion(bf16[2,128,2048]{2,1,0:T(8,128)(2,1)S(1)} %dot_general.39, bf16[2048,1024,1]{1,0,2:T(8,128)(2,1)} %bitcast.63), kind=kOutput, calls=%fused_computation.14 | convolution fusion | flops 1074003968 | bytes 5767168 | tf_op jit(solution)/shard_map/dot_general | solution.py:103
  (41 shorter events, 0.5 us)
Async XLA Ops:
  6.5 61.1 %all-gather.9.cloned.1.call-start = ((), (), s32[]{:S(2)}) async-start(), calls=%async_computation.1 | async-start | bytes 4718592 | tf_op jit(solution)/shard_map/all_gather | solution.py:79
  9.8 83.1 %all-gather.13.cloned.1.call-start = ((), (), s32[]{:S(2)}) async-start(), calls=%async_computation.3 | async-start | bytes 3145728 | tf_op jit(solution)/shard_map/all_gather | solution.py:51
  67.6 10.7 %copy-start.5 = (bf16[2,128,1024]{2,1,0:T(8,128)(2,1)S(1)}, bf16[2,128,1024]{2,1,0:T(8,128)(2,1)}, u32[]{:S(2)}) copy-start(bf16[2,128,1024]{2,1,0:T(8,128)(2,1)} %param.5) | copy-start | bytes 1572868
  73.0 2.7 %copy-start.1 = (f32[16,128,2,6,64]{1,4,3,2,0:T(8,128)}, f32[16,128,2,6,64]{1,4,3,2,0:T(8,128)S(1)}, u32[]{:S(2)}) copy-start(f32[16,128,2,6,64]{1,4,3,2,0:T(8,128)S(1)} %get-tuple-element.14) | copy-start | bytes 18874372
  73.0 3.7 %copy-start.6 = (bf16[16,128,2,6,64]{1,4,3,2,0:T(8,128)(2,1)}, bf16[16,128,2,6,64]{1,4,3,2,0:T(8,128)(2,1)S(1)}, u32[]{:S(2)}) copy-start(bf16[16,128,2,6,64]{1,4,3,2,0:T(8,128)(2,1)S(1)} %get-tuple-element.13) | copy-start | bytes 9437188
  78.3 51.0 %all-gather.17.cloned.1.call-start = ((), (), s32[]{:S(2)}) async-start(), calls=%async_computation.5 | async-start | bytes 2621440 | tf_op jit(solution)/shard_map/all_gather | solution.py:56
  78.4 17.2 %collective-permute-start = (bf16[2,128,512]{2,1,0:T(8,128)(2,1)S(1)}, bf16[2,128,512]{2,1,0:T(8,128)(2,1)S(1)}, u32[]{:S(2)}, u32[]{:S(2)}) collective-permute-start(bf16[2,128,512]{2,1,0:T(8,128)(2,1)S(1)} %constant_dynamic-slice_fusion.1), channel_id=1, source_target_pairs={{0,1},{1,2},{2,3},{3,4},{4,5},{5,6},{6,7},{7,0},{8,9},{9,10},{10,1... | collective-permute-start | bytes 786440 | tf_op jit(solution)/shard_map/ppermute | solution.py:16
  95.5 73.1 %all-gather.15.cloned.1.call-start = ((), (), s32[]{:S(2)}) async-start(), calls=%async_computation.4 | async-start | bytes 2621440 | tf_op jit(solution)/shard_map/all_gather | solution.py:58
  95.6 10.2 %collective-permute-start.1 = (bf16[2,128,512]{2,1,0:T(8,128)(2,1)S(1)}, bf16[2,128,512]{2,1,0:T(8,128)(2,1)S(1)}, u32[]{:S(2)}, u32[]{:S(2)}) collective-permute-start(bf16[2,128,512]{2,1,0:T(8,128)(2,1)S(1)} %collective-permute-done), channel_id=1, source_target_pairs={{0,1},{1,2},{2,3},{3,4},{4,5},{5,6},{6,7},{7,0},{8,9},{9,10},{10,1... | collective-permute-start | bytes 786440 | tf_op jit(solution)/shard_map/ppermute | solution.py:16
  97.2 8.5 %collective-permute-start.4 = (bf16[2,128,512]{2,1,0:T(8,128)(2,1)S(1)}, bf16[2,128,512]{2,1,0:T(8,128)(2,1)S(1)}, u32[]{:S(2)}, u32[]{:S(2)}) collective-permute-start(bf16[2,128,512]{2,1,0:T(8,128)(2,1)S(1)} %constant_dynamic-slice_fusion.1), channel_id=1, source_target_pairs={{0,7},{1,0},{2,1},{3,2},{4,3},{5,4},{6,5},{7,6},{8,15},{9,8},{10,9... | collective-permute-start | bytes 786440 | tf_op jit(solution)/shard_map/ppermute | solution.py:18
  105.7 9.1 %collective-permute-start.2 = (bf16[2,128,512]{2,1,0:T(8,128)(2,1)S(1)}, bf16[2,128,512]{2,1,0:T(8,128)(2,1)S(1)}, u32[]{:S(2)}, u32[]{:S(2)}) collective-permute-start(bf16[2,128,512]{2,1,0:T(8,128)(2,1)S(1)} %collective-permute-done.1), channel_id=1, source_target_pairs={{0,1},{1,2},{2,3},{3,4},{4,5},{5,6},{6,7},{7,0},{8,9},{9,10},{10,1... | collective-permute-start | bytes 786440 | tf_op jit(solution)/shard_map/ppermute | solution.py:16
  105.7 9.2 %collective-permute-start.5 = (bf16[2,128,512]{2,1,0:T(8,128)(2,1)S(1)}, bf16[2,128,512]{2,1,0:T(8,128)(2,1)S(1)}, u32[]{:S(2)}, u32[]{:S(2)}) collective-permute-start(bf16[2,128,512]{2,1,0:T(8,128)(2,1)S(1)} %collective-permute-done.4), channel_id=1, source_target_pairs={{0,7},{1,0},{2,1},{3,2},{4,3},{5,4},{6,5},{7,6},{8,15},{9,8},{10,9... | collective-permute-start | bytes 786440 | tf_op jit(solution)/shard_map/ppermute | solution.py:18
  114.8 8.3 %collective-permute-start.3 = (bf16[2,128,512]{2,1,0:T(8,128)(2,1)S(1)}, bf16[2,128,512]{2,1,0:T(8,128)(2,1)S(1)}, u32[]{:S(2)}, u32[]{:S(2)}) collective-permute-start(bf16[2,128,512]{2,1,0:T(8,128)(2,1)S(1)} %collective-permute-done.2), channel_id=1, source_target_pairs={{0,1},{1,2},{2,3},{3,4},{4,5},{5,6},{6,7},{7,0},{8,9},{9,10},{10,1... | collective-permute-start | bytes 786440 | tf_op jit(solution)/shard_map/ppermute | solution.py:16
  114.9 19.9 %collective-permute-start.6 = (bf16[2,128,512]{2,1,0:T(8,128)(2,1)S(1)}, bf16[2,128,512]{2,1,0:T(8,128)(2,1)S(1)}, u32[]{:S(2)}, u32[]{:S(2)}) collective-permute-start(bf16[2,128,512]{2,1,0:T(8,128)(2,1)S(1)} %collective-permute-done.5), channel_id=1, source_target_pairs={{0,7},{1,0},{2,1},{3,2},{4,3},{5,4},{6,5},{7,6},{8,15},{9,8},{10,9... | collective-permute-start | bytes 786440 | tf_op jit(solution)/shard_map/ppermute | solution.py:18
  132.4 85.6 %all-gather.11.cloned.1.call-start = ((), (), s32[]{:S(2)}) async-start(), calls=%async_computation.2 | async-start | bytes 6291456 | tf_op jit(solution)/shard_map/all_gather | solution.py:74
  164.5 6.1 %copy-start.3 = (f32[8,2,64,64]{3,2,1,0:T(8,128)S(1)}, f32[8,2,64,64]{3,2,1,0:T(8,128)}, u32[]{:S(2)}) copy-start(f32[8,2,64,64]{3,2,1,0:T(8,128)} %get-tuple-element.7) | copy-start | bytes 786436
  164.5 9.1 %copy-start = (f32[32,2,64,64]{3,2,1,0:T(8,128)S(1)}, f32[32,2,64,64]{3,2,1,0:T(8,128)}, u32[]{:S(2)}) copy-start(f32[32,2,64,64]{3,2,1,0:T(8,128)} %all-gather.13.cloned.1.call-done) | copy-start | bytes 3145732
  170.6 5.6 %copy-start.2 = (f32[16,2,128,128]{3,2,1,0:T(8,128)S(1)}, f32[16,2,128,128]{3,2,1,0:T(8,128)}, u32[]{:S(2)}) copy-start(f32[16,2,128,128]{3,2,1,0:T(8,128)} %fusion.37) | copy-start | bytes 6291460
  176.2 3.5 %copy-start.4 = (bf16[128,2,64,16]{0,2,1,3:T(8,128)(2,1)S(1)}, bf16[128,2,64,16]{0,2,1,3:T(8,128)(2,1)}, u32[]{:S(2)}) copy-start(bf16[128,2,64,16]{0,2,1,3:T(8,128)(2,1)} %copy.48) | copy-start | bytes 1572868
Sparse Core Ops, SparseCore 0:
  9.9 57.6 all-gather.8
  78.4 14.5 all-gather.12
  95.6 33.6 all-gather.16
  132.6 34.3 all-gather.14
  168.6 19.0 all-gather.10
